TPU v7x, 512 devices: a whole 4x4x16 slice. The times are simulated.
512 devices in a mesh: context: 128 (over z, y, core), tensor: 4 (over x).
Axes of the slice: x: 4, y: 4, z: 16, core: 2. Of those that a mesh axis runs over, the one named last changes fastest.
Arguments:
- projected: bfloat16 [3, 16, 512, 16384], P(None, 'tensor', None, 'context'), may hold values from -6 to 6
- long_filter: bfloat16 [512, 128], replicated, may hold values from -0.5 to 0.5
- cotangent: bfloat16 [16, 512, 16384], P('tensor', None, 'context'), may hold values from -6 to 6
Outputs:
- mixed: bfloat16 [16, 512, 16384], P('tensor', None, 'context')
- stream_grads: bfloat16 [3, 16, 512, 16384], P(None, 'tensor', None, 'context')
- filter_grads: float32 [512, 128], P('context')
All inputs are finite; a program needn't handle non-finite values.
Results may differ from a plain program's by a relative error of at most 0.0057.
Values may be sent and summed in bfloat16 or wider, within the bound.
No kernel may reach another device: no remote copies, remote signals or barrier semaphores. Data moves between devices by JAX's collectives and lax.ppermute only.
A program may use at most 64 MiB of HBM per device.

v0:
```python
import math
import jax
import jax.numpy as jnp
from jax import lax
from jax.sharding import PartitionSpec as P


def selector_table(filter_taps):
    rows = lax.broadcasted_iota(jnp.int32, (filter_taps, filter_taps), 0)
    cols = lax.broadcasted_iota(jnp.int32, (filter_taps, filter_taps), 1)
    offset = (rows - cols + filter_taps) % filter_taps
    taps = lax.broadcasted_iota(jnp.int32, (filter_taps, filter_taps, filter_taps), 0)
    table = (offset[None, :, :] == taps).astype(jnp.bfloat16)
    return (table.reshape(filter_taps, filter_taps * filter_taps), rows >= cols)


def conv_both(tiles, earlier, grad_tiles, grad_next, filters):
    groups, filter_taps = filters.shape
    block_width = math.gcd(groups, 32)
    table, lower = selector_table(filter_taps)
    table_wide = table.astype(jnp.float32)

    def advance(index, carry):
        circulant = jnp.dot(filters, table, preferred_element_type=jnp.float32).reshape(
            block_width, filter_taps, filter_taps
        )
        low_band = jnp.where(lower[None], circulant, 0.0).astype(jnp.bfloat16)
        high_band = jnp.where(lower[None], 0.0, circulant).astype(jnp.bfloat16)
        forward = jnp.einsum("mgbk,gik->mgbi", tiles, low_band, preferred_element_type=jnp.float32)
        forward = forward + jnp.einsum(
            "mgbk,gik->mgbi", earlier, high_band, preferred_element_type=jnp.float32
        )
        backward = jnp.einsum(
            "mgbi,gik->mgbk", grad_tiles, low_band, preferred_element_type=jnp.float32
        )
        backward = backward + jnp.einsum(
            "mgbi,gik->mgbk", grad_next, high_band, preferred_element_type=jnp.float32
        )
        outer_low = jnp.einsum(
            "mgbi,mgbk->gik", grad_tiles, tiles, preferred_element_type=jnp.float32
        )
        outer_high = jnp.einsum(
            "mgbi,mgbk->gik", grad_tiles, earlier, preferred_element_type=jnp.float32
        )
        merged = jnp.where(lower[None], outer_low, outer_high).reshape(
            block_width, filter_taps * filter_taps
        )
        sums = jnp.dot(merged, table_wide.T, precision=lax.Precision.HIGHEST)
        filtered_out = forward.astype(jnp.bfloat16)
        grads_out = backward.astype(jnp.bfloat16)
        return (filtered_out, grads_out, sums)

    initial = (
        jnp.zeros(tiles.shape, jnp.bfloat16),
        jnp.zeros(tiles.shape, jnp.bfloat16),
        jnp.zeros((groups, filter_taps), jnp.float32),
    )
    return lax.fori_loop(0, groups // block_width, advance, initial)


def shifted_tiles(tiles, before, grad_tiles, after):
    earlier = jnp.concatenate([before, tiles[:, :, :-1]], 2)
    grad_next = jnp.concatenate([grad_tiles[:, :, 1:], after], 2)
    return (earlier, grad_next)


def channel_filters(long_filter, own_groups):
    first_group = lax.axis_index("context") * own_groups
    return lax.dynamic_slice_in_dim(long_filter, first_group, own_groups, 0)


def channel_conv(columns, grad_columns, long_filter, filter_taps):
    members, own_groups, length = columns.shape
    filters = channel_filters(long_filter, own_groups)
    tiles = columns.reshape(members, own_groups, length // filter_taps, filter_taps)
    grad_tiles = grad_columns.reshape(members, own_groups, length // filter_taps, filter_taps)
    blank = jnp.zeros((members, own_groups, 1, filter_taps), jnp.bfloat16)
    earlier, grad_next = shifted_tiles(tiles, blank, grad_tiles, blank)
    filtered_tiles, gated_tiles, partial_taps = conv_both(
        tiles, earlier, grad_tiles, grad_next, filters
    )
    return (
        filtered_tiles.reshape(members, own_groups, length),
        gated_tiles.reshape(members, own_groups, length),
        partial_taps,
    )


def body(projected, long_filter, cotangent):
    filter_taps = long_filter.shape[1]
    query_stream = projected[0]
    key_stream = projected[1]
    value_stream = projected[2]
    gated = (key_stream.astype(jnp.float32) * value_stream.astype(jnp.float32)).astype(jnp.bfloat16)
    members, groups, local_tokens = gated.shape
    length = local_tokens * lax.axis_size("context")
    factor = 1.0 / math.sqrt(members * lax.axis_size("tensor") * length)
    grad_filtered = (cotangent.astype(jnp.float32) * query_stream.astype(jnp.float32)).astype(
        jnp.bfloat16
    )
    columns = lax.all_to_all(gated, "context", split_axis=1, concat_axis=2, tiled=True)
    grad_columns = lax.all_to_all(grad_filtered, "context", split_axis=1, concat_axis=2, tiled=True)
    filtered_columns, gated_columns, partial_taps = channel_conv(
        columns, grad_columns, long_filter, filter_taps
    )
    filtered = lax.all_to_all(filtered_columns, "context", split_axis=2, concat_axis=1, tiled=True)
    grad_gated = lax.all_to_all(gated_columns, "context", split_axis=2, concat_axis=1, tiled=True)
    filter_grads = lax.psum(partial_taps, "tensor") * factor
    filtered_wide = filtered.astype(jnp.float32)
    grad_wide = grad_gated.astype(jnp.float32)
    mixed = (query_stream.astype(jnp.float32) * filtered_wide).astype(jnp.bfloat16)
    stream_grads = jnp.stack(
        [
            cotangent.astype(jnp.float32) * filtered_wide,
            grad_wide * value_stream.astype(jnp.float32),
            grad_wide * key_stream.astype(jnp.float32),
        ]
    ).astype(jnp.bfloat16)
    return (mixed, stream_grads, filter_grads)


def solution(mesh):
    in_specs = (P(None, "tensor", None, "context"), P(), P("tensor", None, "context"))
    out_specs = (
        P("tensor", None, "context"),
        P(None, "tensor", None, "context"),
        P("context", None),
    )
    return jax.shard_map(body, mesh=mesh, in_specs=in_specs, out_specs=out_specs, check_vma=False)
```

profile of v0, /device:TPU:39, one launch (start us, length us, event | category | flops | bytes accessed | tf_op | source)
XLA Modules:
  0.0 418.9 jit_solution(2552468281968310351)
XLA Ops:
  0.6 2.3 fusion.32
  2.9 1.5 fusion.15
  4.4 19.5 %all-to-all-start = ((bf16[4,512,128]{2,0,1:T(4,128)(2,1)}), bf16[4,512,128]{2,0,1:T(4,128)(2,1)S(1)}, u32[]{:S(2)}, u32[]{:S(2)}) async-start(bf16[4,512,128]{2,0,1:T(4,128)(2,1)} %fusion.15), calls=%async_computation | async-start | bytes 1048576 | tf_op jit(solution)/shard_map/all_to_all | solution.py:101
  24.0 3.7 fusion.21
  28.0 29.5 %all-to-all-done = bf16[4,512,128]{2,0,1:T(4,128)(2,1)S(1)} async-done(((bf16[4,512,128]{2,0,1:T(4,128)(2,1)}), bf16[4,512,128]{2,0,1:T(4,128)(2,1)S(1)}, u32[]{:S(2)}, u32[]{:S(2)}) %all-to-all-start) | async-done | bytes 524320 | tf_op jit(solution)/shard_map/all_to_all | solution.py:101
  58.3 26.7 %copy.58 = bf16[4,4,128,128]{1,0,3,2:T(4,128)(2,1)} copy(bf16[4,4,128,128]{2,3,0,1:T(8,128)(2,1)S(1)} %fusion.7) | data formatting | bytes 1048576 | tf_op jit(solution)/shard_map/reshape | solution.py:83
  85.1 31.2 %reshape.98 = bf16[128,2,1024]{2,1,0:T(2,128)(2,1)S(1)} reshape(bf16[16384,4,4]{2,1,0:T(4,128)(2,1)} %bitcast.75) | data formatting | bytes 1048576
  116.2 39.7 %all_to_all.48 = bf16[128,2,1024]{2,1,0:T(2,128)(2,1)S(1)} all-to-all(bf16[128,2,1024]{2,1,0:T(2,128)(2,1)S(1)} %reshape.98), channel_id=1, replica_groups=mesh['context'=128,'tensor'=4] {'context'}, dimensions={0} | all-to-all | bytes 1048576 | tf_op jit(solution)/shard_map/all_to_all | solution.py:106
  156.0 37.0 %reshape.99 = bf16[16384,4,4]{2,1,0:T(4,128)(2,1)} reshape(bf16[128,2,1024]{2,1,0:T(2,128)(2,1)S(1)} %all_to_all.48) | data formatting | bytes 1048576
  193.0 21.7 %copy.29 = f32[4,4,128,128]{3,0,1,2:T(4,128)} copy(bf16[4,4,128,128]{1,0,3,2:T(4,128)(2,1)} %bitcast.76) | data formatting | bytes 1572864 | tf_op jit(solution)/shard_map/convert_element_type | solution.py:109
  214.7 3.2 fusion.12
  217.9 39.9 %all_to_all.49 = bf16[4,512,128]{2,0,1:T(4,128)(2,1)S(1)} all-to-all(bf16[4,512,128]{2,0,1:T(4,128)(2,1)S(1)} %get-tuple-element.32), channel_id=1, replica_groups=mesh['context'=128,'tensor'=4] {'context'}, dimensions={1} | all-to-all | bytes 1048576 | tf_op jit(solution)/shard_map/all_to_all | solution.py:102
  258.7 26.7 %copy.65 = bf16[4,4,128,128]{1,0,3,2:T(4,128)(2,1)} copy(bf16[4,4,128,128]{2,3,0,1:T(8,128)(2,1)S(1)} %fusion.6) | data formatting | bytes 1048576 | tf_op jit(solution)/shard_map/reshape | solution.py:84
  285.4 31.8 %reshape.100 = bf16[128,2,1024]{2,1,0:T(2,128)(2,1)} reshape(bf16[16384,4,4]{2,1,0:T(4,128)(2,1)} %bitcast.77) | data formatting | bytes 1048576
  317.2 6.3 %all-to-all-start.3 = ((bf16[128,2,1024]{2,1,0:T(2,128)(2,1)}), bf16[128,2,1024]{2,1,0:T(2,128)(2,1)S(1)}, u32[]{:S(2)}, u32[]{:S(2)}) async-start(bf16[128,2,1024]{2,1,0:T(2,128)(2,1)} %reshape.100), calls=%async_computation.3 | async-start | bytes 1048576 | tf_op jit(solution)/shard_map/all_to_all | solution.py:107
  323.6 1.9 copy.42
  326.2 4.1 fusion.8
  330.4 6.3 %psum.7 = f32[4,128]{1,0:T(4,128)S(1)} all-reduce(f32[4,128]{1,0:T(4,128)S(1)} %fusion.8), channel_id=1, replica_groups=mesh['context'=128,'tensor'=4] {'tensor'}, use_global_device_ids=true, to_apply=%region_0.1 | all-reduce | flops 512 | bytes 4096 | tf_op jit(solution)/shard_map/psum | solution.py:108
  337.2 20.0 %all-to-all-done.3 = bf16[128,2,1024]{2,1,0:T(2,128)(2,1)S(1)} async-done(((bf16[128,2,1024]{2,1,0:T(2,128)(2,1)}), bf16[128,2,1024]{2,1,0:T(2,128)(2,1)S(1)}, u32[]{:S(2)}, u32[]{:S(2)}) %all-to-all-start.3) | async-done | bytes 524320 | tf_op jit(solution)/shard_map/all_to_all | solution.py:107
  357.2 37.0 %reshape.101 = bf16[16384,4,4]{2,1,0:T(4,128)(2,1)} reshape(bf16[128,2,1024]{2,1,0:T(2,128)(2,1)S(1)} %all-to-all-done.3) | data formatting | bytes 1048576
  394.2 21.0 %copy.37 = f32[4,4,128,128]{3,0,1,2:T(4,128)S(1)} copy(bf16[4,4,128,128]{1,0,3,2:T(4,128)(2,1)} %bitcast.78) | data formatting | bytes 1572864 | tf_op jit(solution)/shard_map/convert_element_type | solution.py:110
  415.2 1.0 fusion.11
  416.2 1.3 pad_maximum_fusion
  417.5 1.4 copy.43
  (24 shorter events, 3.5 us)
Async XLA Ops:
  0.6 23.3 %copy-start = (bf16[512,128]{1,0:T(8,128)(2,1)S(1)}, bf16[512,128]{1,0:T(8,128)(2,1)}, u32[]{:S(2)}) copy-start(bf16[512,128]{1,0:T(8,128)(2,1)} %param.4) | copy-start | bytes 393220
  4.4 53.1 %all-to-all-start = ((bf16[4,512,128]{2,0,1:T(4,128)(2,1)}), bf16[4,512,128]{2,0,1:T(4,128)(2,1)S(1)}, u32[]{:S(2)}, u32[]{:S(2)}) async-start(bf16[4,512,128]{2,0,1:T(4,128)(2,1)} %fusion.15), calls=%async_computation | async-start | bytes 1048576 | tf_op jit(solution)/shard_map/all_to_all | solution.py:101
  193.0 21.7 %copy-start.2 = (bf16[1,4,512,128]{3,2,1,0:T(8,128)(2,1)S(1)}, bf16[1,4,512,128]{3,2,1,0:T(8,128)(2,1)}, u32[]{:S(2)}) copy-start(bf16[1,4,512,128]{3,2,1,0:T(8,128)(2,1)} %get-tuple-element.27) | copy-start | bytes 1572868
  193.0 21.7 %copy-start.4 = (bf16[4,512,128]{2,1,0:T(8,128)(2,1)S(1)}, bf16[4,512,128]{2,1,0:T(8,128)(2,1)}, u32[]{:S(2)}) copy-start(bf16[4,512,128]{2,1,0:T(8,128)(2,1)} %param.5) | copy-start | bytes 1572868
  317.2 39.9 %all-to-all-start.3 = ((bf16[128,2,1024]{2,1,0:T(2,128)(2,1)}), bf16[128,2,1024]{2,1,0:T(2,128)(2,1)S(1)}, u32[]{:S(2)}, u32[]{:S(2)}) async-start(bf16[128,2,1024]{2,1,0:T(2,128)(2,1)} %reshape.100), calls=%async_computation.3 | async-start | bytes 1048576 | tf_op jit(solution)/shard_map/all_to_all | solution.py:107
  415.2 1.0 copy-start.3
  416.2 2.7 copy-start.1
where the time goes:
time: 420 us; the launch traced here: 419 us
  local copies, waits for them, and re-layouts  239 us (57%)
  blocking collectives  85.9 us (20%)
  waiting for transfers between devices  49.5 us (12%)
  starting transfers between devices  25.8 us (6%)
  matrix products  9.88 us (2%)
  other arithmetic  7.57 us (2%)
    unnamed x16, local copies, waits for them, and re-layouts  140 us
    all_to_all x1, blocking collectives, body(): lax.all_to_all(grad_filtered, 'context', split_axis=1, concat_axis=2, til...  39.9 us
    all_to_all x1, blocking collectives, body(): lax.all_to_all(filtered_columns, 'context', split_axis=2, concat_axis=1,...  39.7 us
    all_to_all x1, waiting for transfers between devices, body(): lax.all_to_all(gated, 'context', split_axis=1, concat_axis=2, tiled=True)  29.5 us
    reshape x1, local copies, waits for them, and re-layouts, channel_conv(): filtered_tiles.reshape(members, own_groups, length)  26.7 us
    reshape x1, local copies, waits for them, and re-layouts, channel_conv(): gated_tiles.reshape(members, own_groups, length)  26.7 us
    convert_element_type x1, local copies, waits for them, and re-layouts, body(): filtered_wide = filtered.astype(jnp.float32)  21.7 us
    convert_element_type x1, local copies, waits for them, and re-layouts, body(): grad_wide = grad_gated.astype(jnp.float32)  21 us
  transfers between devices with their start and end apart: 2, of which 2 were waited for; matrix products, arithmetic and copies ran while one was open for 3% of the time, Pallas kernels for 0%

commit v1 on v0

--- a/solution.py
+++ b/solution.py
@@ -3,6 +3,16 @@
 import jax.numpy as jnp
 from jax import lax
 from jax.sharding import PartitionSpec as P
+from jax.lax import all_to_all, axis_size
+
+
+def chunk_push(t0):
+    mixed_arr = axis_size("context")
+    e_now = jnp.split(t0, mixed_arr, axis=2)
+    new = jnp.stack(e_now, axis=0)
+    side_arr = all_to_all(new, "context", 0, 0)
+    finding = jnp.concatenate(side_arr, axis=1)
+    return finding
 
 
 def selector_table(filter_taps):
@@ -104,7 +114,7 @@
         columns, grad_columns, long_filter, filter_taps
     )
     filtered = lax.all_to_all(filtered_columns, "context", split_axis=2, concat_axis=1, tiled=True)
-    grad_gated = lax.all_to_all(gated_columns, "context", split_axis=2, concat_axis=1, tiled=True)
+    grad_gated = chunk_push(gated_columns)
     filter_grads = lax.psum(partial_taps, "tensor") * factor
     filtered_wide = filtered.astype(jnp.float32)
     grad_wide = grad_gated.astype(jnp.float32)

time: 420 us -> 306 us (0.73)
  the two profiles are of different devices: /device:TPU:39 before, /device:TPU:35 now
where the time goes in v1:
time: 306 us; the launch traced here: 305 us
  local copies, waits for them, and re-layouts  124 us (41%)
  blocking collectives  86.8 us (28%)
  waiting for transfers between devices  49.9 us (16%)
  starting transfers between devices  26.4 us (9%)
  matrix products  10.7 us (3%)
  other arithmetic  5.77 us (2%)
    unnamed x143, local copies, waits for them, and re-layouts  72.7 us
    all_to_all x1, blocking collectives, chunk_push(): side_arr = all_to_all(new, 'context', 0, 0)  39.7 us
    all_to_all x1, blocking collectives, body(): lax.all_to_all(gated, 'context', split_axis=1, concat_axis=2, tiled=True)  39.7 us
    all_to_all x1, waiting for transfers between devices, body(): lax.all_to_all(grad_filtered, 'context', split_axis=1, concat_axis=2, til...  29.5 us
    reshape x1, local copies, waits for them, and re-layouts, channel_conv(): filtered_tiles.reshape(members, own_groups, length)  27.3 us
    convert_element_type x1, local copies, waits for them, and re-layouts, body(): filtered_wide = filtered.astype(jnp.float32)  21.1 us
    all_to_all x1, waiting for transfers between devices, body(): lax.all_to_all(filtered_columns, 'context', split_axis=2, concat_axis=1,...  20.4 us
    all_to_all x1, starting transfers between devices, body(): lax.all_to_all(grad_filtered, 'context', split_axis=1, concat_axis=2, til...  19.5 us
  transfers between devices with their start and end apart: 2, of which 2 were waited for; matrix products, arithmetic and copies ran while one was open for 3% of the time, Pallas kernels for 0%

profile of v1, /device:TPU:35, one launch (start us, length us, event | category | flops | bytes accessed | tf_op | source)
XLA Modules:
  0.0 304.9 jit_solution(11914550479397500090)
XLA Ops:
  0.6 1.4 fusion.14
  2.0 1.2 copy.177
  3.2 19.5 %all-to-all-start.2 = ((bf16[4,512,128]{2,0,1:T(4,128)(2,1)}), bf16[4,512,128]{2,0,1:T(4,128)(2,1)S(1)}, u32[]{:S(2)}, u32[]{:S(2)}) async-start(bf16[4,512,128]{2,0,1:T(4,128)(2,1)} %copy.177), calls=%async_computation.2 | async-start | bytes 1048576 | tf_op jit(solution)/shard_map/all_to_all | solution.py:112
  22.8 3.7 %fusion.22 = (bf16[4,128,128,1]{2,0,1,3:T(4,128)(2,1)S(1)}, bf16[4,128,128,1]{2,0,1,3:T(4,128)(2,1)S(1)}) fusion(pred[128,128]{1,0:T(8,128)(4,1)S(1)} %iota_compare_fusion.6, s32[128,128]{1,0:T(8,128)S(1)} %add_select_fusion, bf16[512,128]{1,0:T(8,128)(2,1)S(1)} %copy-done, s32[]{:T(128)S(6)} %select_n.33), kind=kOutput, calls=%fused_computation.169 | convolution fusion | flops 19005440 | bytes 345092 | tf_op jit(solution)/shard_map/while/body/eval_jaxpr/dot_general | solution.py:34
  26.8 29.5 %all-to-all-done.2 = bf16[4,512,128]{2,0,1:T(4,128)(2,1)S(1)} async-done(((bf16[4,512,128]{2,0,1:T(4,128)(2,1)}), bf16[4,512,128]{2,0,1:T(4,128)(2,1)S(1)}, u32[]{:S(2)}, u32[]{:S(2)}) %all-to-all-start.2) | async-done | bytes 524320 | tf_op jit(solution)/shard_map/all_to_all | solution.py:112
  59.7 39.7 %all_to_all.44 = bf16[128,4,4,128]{3,2,1,0:T(4,128)(2,1)S(1)} all-to-all(bf16[128,4,4,128]{3,2,1,0:T(4,128)(2,1)S(1)} %constant_dynamic-update-slice_fusion), channel_id=1, replica_groups=mesh['context'=128,'tensor'=4] {'context'}, dimensions={0} | all-to-all | bytes 1048576 | tf_op jit(solution)/shard_map/all_to_all | solution.py:13
  99.8 1.1 copy-done.1
  100.8 1.3 fusion.11
  102.2 0.4 copy.169
  102.6 39.7 %all_to_all.45 = bf16[4,512,128]{2,0,1:T(4,128)(2,1)S(1)} all-to-all(bf16[4,512,128]{2,0,1:T(4,128)(2,1)S(1)} %copy.169), channel_id=1, replica_groups=mesh['context'=128,'tensor'=4] {'context'}, dimensions={1} | all-to-all | bytes 1048576 | tf_op jit(solution)/shard_map/all_to_all | solution.py:111
  142.4 0.3 fusion.31
  142.8 1.1 fusion.7
  143.9 27.3 %copy.202 = bf16[4,4,128,128]{1,0,3,2:T(4,128)(2,1)} copy(bf16[4,4,128,128]{2,3,0,1:T(8,128)(2,1)} %fusion.7) | data formatting | bytes 1048576 | tf_op jit(solution)/shard_map/reshape | solution.py:93
  171.3 31.8 %reshape.97 = bf16[128,2,1024]{2,1,0:T(2,128)(2,1)} reshape(bf16[16384,4,4]{2,1,0:T(4,128)(2,1)} %bitcast.578) | data formatting | bytes 1048576
  203.1 6.9 %all-to-all-start.1 = ((bf16[128,2,1024]{2,1,0:T(2,128)(2,1)}), bf16[128,2,1024]{2,1,0:T(2,128)(2,1)}, u32[]{:S(2)}, u32[]{:S(2)}) async-start(bf16[128,2,1024]{2,1,0:T(2,128)(2,1)} %reshape.97), calls=%async_computation.1 | async-start | bytes 1048576 | tf_op jit(solution)/shard_map/all_to_all | solution.py:116
  210.1 0.4 convolution_bitcast_fusion
  210.8 4.1 %fusion.8 = f32[4,128]{1,0:T(4,128)S(1)} fusion(s32[128,128]{1,0:T(8,128)S(1)} %copy-done.6, f32[4,128,128]{2,1,0:T(8,128)S(1)} %convolution_bitcast_fusion, f32[4,128,128]{2,1,0:T(8,128)S(1)} %convolution_bitcast_fusion.1, pred[128,128]{1,0:T(8,128)(4,1)S(1)} %iota_compare_fusion.6), kind=kOutput, calls=%fused_computation.21 | convolution fusion | flops 102825984 | bytes 608256 | tf_op jit(solution)/shard_map/while/body/eval_jaxpr/dot_general | solution.py:58
  215.0 7.4 %psum.7 = f32[4,128]{1,0:T(4,128)S(1)} all-reduce(f32[4,128]{1,0:T(4,128)S(1)} %fusion.8), channel_id=1, replica_groups=mesh['context'=128,'tensor'=4] {'tensor'}, use_global_device_ids=true, to_apply=%region_0.1 | all-reduce | flops 512 | bytes 4096 | tf_op jit(solution)/shard_map/psum | solution.py:118
  222.3 0.6 broadcast_multiply_fusion
  222.9 20.4 %all-to-all-done.1 = bf16[128,2,1024]{2,1,0:T(2,128)(2,1)} async-done(((bf16[128,2,1024]{2,1,0:T(2,128)(2,1)}), bf16[128,2,1024]{2,1,0:T(2,128)(2,1)}, u32[]{:S(2)}, u32[]{:S(2)}) %all-to-all-start.1) | async-done | bytes 524320 | tf_op jit(solution)/shard_map/all_to_all | solution.py:116
  243.3 37.8 %reshape.98 = bf16[16384,4,4]{2,1,0:T(4,128)(2,1)} reshape(bf16[128,2,1024]{2,1,0:T(2,128)(2,1)} %all-to-all-done.1) | data formatting | bytes 1048576
  281.1 21.1 %copy.176 = f32[4,4,128,128]{3,1,2,0:T(4,128)S(1)} copy(bf16[4,4,128,128]{1,0,3,2:T(4,128)(2,1)} %bitcast.579) | data formatting | bytes 1572864 | tf_op jit(solution)/shard_map/convert_element_type | solution.py:119
  302.2 1.0 fusion.15
  303.5 1.3 pad_maximum_fusion
  (155 shorter events, 4.4 us)
Async XLA Ops:
  0.6 22.1 %copy-start = (bf16[512,128]{1,0:T(8,128)(2,1)S(1)}, bf16[512,128]{1,0:T(8,128)(2,1)}, u32[]{:S(2)}) copy-start(bf16[512,128]{1,0:T(8,128)(2,1)} %param.4) | copy-start | bytes 393220
  3.2 53.1 %all-to-all-start.2 = ((bf16[4,512,128]{2,0,1:T(4,128)(2,1)}), bf16[4,512,128]{2,0,1:T(4,128)(2,1)S(1)}, u32[]{:S(2)}, u32[]{:S(2)}) async-start(bf16[4,512,128]{2,0,1:T(4,128)(2,1)} %copy.177), calls=%async_computation.2 | async-start | bytes 1048576 | tf_op jit(solution)/shard_map/all_to_all | solution.py:112
  22.8 33.7 %copy-start.5 = (s32[128,128]{1,0:T(8,128)}, s32[128,128]{1,0:T(8,128)S(1)}, u32[]{:S(2)}) copy-start(s32[128,128]{1,0:T(8,128)S(1)} %add_select_fusion) | copy-start | bytes 196612
  99.4 1.4 copy-start.1
  203.1 7.7 %copy-start.6 = (s32[128,128]{1,0:T(8,128)S(1)}, s32[128,128]{1,0:T(8,128)}, u32[]{:S(2)}) copy-start(s32[128,128]{1,0:T(8,128)} %copy-done.5) | copy-start | bytes 196612
  203.1 40.2 %all-to-all-start.1 = ((bf16[128,2,1024]{2,1,0:T(2,128)(2,1)}), bf16[128,2,1024]{2,1,0:T(2,128)(2,1)}, u32[]{:S(2)}, u32[]{:S(2)}) async-start(bf16[128,2,1024]{2,1,0:T(2,128)(2,1)} %reshape.97), calls=%async_computation.1 | async-start | bytes 1048576 | tf_op jit(solution)/shard_map/all_to_all | solution.py:116
  281.1 21.1 %copy-start.2 = (bf16[4,512,128]{2,1,0:T(8,128)(2,1)S(1)}, bf16[4,512,128]{2,1,0:T(8,128)(2,1)}, u32[]{:S(2)}) copy-start(bf16[4,512,128]{2,1,0:T(8,128)(2,1)} %param.5) | copy-start | bytes 1572868
  302.2 1.0 copy-start.3
  302.2 1.3 copy-start.4
